TPU v7x, 512 devices: a whole 4x8x8 slice. The times are simulated.
512 devices in a mesh: req: 64 (over x, z, core), mdl: 8 (over y).
Axes of the slice: x: 4, y: 8, z: 8, core: 2. Of those that a mesh axis runs over, the one named last changes fastest.
Arguments:
- queries: bfloat16 [1536, 2048], P('req', 'mdl'), may hold values from -6 to 6
- scored_key_value: bfloat16 [2, 1536, 1024], P(None, 'req', 'mdl'), may hold values from -6 to 6
- gate_logits: bfloat16 [1536, 2048], P('req', 'mdl'), may hold values from -8 to 8
- page_kv: bfloat16 [2, 2176, 128, 1024], P(None, 'req', None, 'mdl'), may hold values from -6 to 6
- page_table: int32 [64, 128], replicated, may hold values from -1 to 2175, as said below
- lengths: int32 [64], replicated, may hold values from 1 to 16384
- assignment: int32 [64], replicated, may hold values from 0 to 63, each once
- offsets: int32 [64, 24], P('req'), may hold values from 0 to 23, each once within a row
- residual: bfloat16 [1536, 2048], P('req'), may hold values from -18 to 18
- out_weight: bfloat16 [2048, 2048], P('mdl'), may hold values from -1 to 1
- norm_gain: bfloat16 [2048], replicated, may hold values from 0.5 to 1.5
- head_weight: bfloat16 [2048, 131072], P(None, ('req', 'mdl')), may hold values from -0.3193592 to 0.3193592
- targets: int32 [1536], replicated, may hold values from 0 to 131071
Outputs:
- logprob: float32 [1536], P('req')
- entropy: float32 [1536], P('req')
Inputs may be any that keep to these rules, and one draw needn't show every extreme that they name: `page_table`: row i lists the pages of request i in order, each as owner index times 34 plus a slot, followed by -1. Request i has ceil(lengths[i] / 128) pages, no page serves two requests, and at most 2 pages of one request sit on one owner. `assignment`: each index along req holds exactly one request. `offsets`: each row is an order of 0 to 23.
All inputs are finite; a program needn't handle non-finite values.
Results may differ from a plain program's by a relative error of at most 0.0013.
Values may be sent and summed in bfloat16 or wider, within the bound.
No kernel may reach another device: no remote copies, remote signals or barrier semaphores. Data moves between devices by JAX's collectives and lax.ppermute only.
A program may use at most 128 MiB of HBM per device.

v0:
```python
import jax
import jax.numpy as jnp
from jax import lax
from jax.sharding import PartitionSpec as P

HEAD_SIZE = 128
CAP = 2
FLOOR_SCORE = -1e30
NORM_EPSILON = 1e-06


def body(
    queries,
    scored_key_value,
    gate_logits,
    page_kv,
    page_table,
    lengths,
    assignment,
    offsets,
    residual,
    out_weight,
    norm_gain,
    head_weight,
    targets,
):
    groups = lax.axis_size("req")
    req_index = lax.axis_index("req")
    fresh_count = queries.shape[0]
    kv_heads = scored_key_value.shape[2] // HEAD_SIZE
    queries_per_group = queries.shape[1] // scored_key_value.shape[2]
    page_len = page_kv.shape[2]
    store_pages = page_kv.shape[1]
    page_slots = page_table.shape[1]
    score_scale = HEAD_SIZE ** (-0.5)
    indices = jnp.arange(groups, dtype=jnp.int32)
    holder = jnp.sum(
        jnp.where(assignment[:, None] == indices[None, :], indices[:, None], 0), axis=0
    )
    query_heads = queries.reshape(fresh_count, kv_heads, queries_per_group, HEAD_SIZE)
    scored_keys = scored_key_value[0].reshape(fresh_count, kv_heads, HEAD_SIZE)
    scored_values = scored_key_value[1].reshape(fresh_count, kv_heads, HEAD_SIZE)
    fresh_order = offsets[0]
    visible = fresh_order[None, :] <= fresh_order[:, None]
    fresh_scores = (
        jnp.einsum("tjgd,ujd->jgtu", query_heads, scored_keys, preferred_element_type=jnp.float32)
        * score_scale
    )
    fresh_scores = jnp.where(visible[None, None], fresh_scores, FLOOR_SCORE)
    fresh_top = jnp.max(fresh_scores, axis=-1)
    page_owner = jnp.where(page_table >= 0, page_table // store_pages, -1)
    page_slot = page_table % store_pages
    is_mine = page_owner == req_index
    page_rank = jnp.cumsum(is_mine.astype(jnp.int32), axis=1) - 1
    slot_picks = [
        jnp.sum(jnp.where(is_mine & (page_rank == cap_index), page_slot, 0), axis=1)
        for cap_index in range(CAP)
    ]
    send_slot = jnp.take(jnp.stack(slot_picks, axis=1), holder, axis=0).reshape(-1)
    outgoing = jnp.take(page_kv, send_slot, axis=1)
    arrived = lax.all_to_all(outgoing, "req", split_axis=1, concat_axis=1, tiled=True)
    request = holder[req_index]
    page_table_row = jnp.take(page_table, request, axis=0)
    length = jnp.take(lengths, request)
    row_owner = jnp.where(page_table_row >= 0, page_table_row // store_pages, -1)
    source = row_owner[None, :] == indices[:, None]
    row_rank = jnp.cumsum(source.astype(jnp.int32), axis=1) - 1
    page_fill = jnp.clip(length - jnp.arange(page_slots, dtype=jnp.int32) * page_len, 0, page_len)
    counts = jnp.stack(
        [
            jnp.sum(jnp.where(source & (row_rank == cap_index), page_fill[None, :], 0), axis=1)
            for cap_index in range(CAP)
        ],
        axis=1,
    ).reshape(-1)
    live_keys = (jnp.arange(page_len, dtype=jnp.int32)[None, :] < counts[:, None]).reshape(-1)
    cached_keys = arrived[0].reshape(-1, kv_heads, HEAD_SIZE)
    cached_values = arrived[1].reshape(-1, kv_heads, HEAD_SIZE)
    scores = (
        jnp.einsum("tjgd,ljd->jgtl", query_heads, cached_keys, preferred_element_type=jnp.float32)
        * score_scale
    )
    scores = jnp.where(live_keys[None, None, None, :], scores, FLOOR_SCORE)
    row_top = jnp.maximum(jnp.max(scores, axis=-1), fresh_top)
    weights = jnp.exp(scores - row_top[..., None])
    weight_sum = jnp.sum(weights, axis=-1)
    summed = jnp.einsum(
        "jgtl,ljd->tjgd",
        weights.astype(jnp.bfloat16),
        cached_values,
        preferred_element_type=jnp.float32,
    )
    fresh_weights = jnp.exp(fresh_scores - row_top[..., None])
    weight_sum = weight_sum + jnp.sum(fresh_weights, axis=-1)
    summed = summed + jnp.einsum(
        "jgtu,ujd->tjgd",
        fresh_weights.astype(jnp.bfloat16),
        scored_values,
        preferred_element_type=jnp.float32,
    )
    attended = summed / jnp.transpose(weight_sum, (2, 0, 1))[..., None]
    gated_out = (
        attended.reshape(fresh_count, -1) * jax.nn.sigmoid(gate_logits.astype(jnp.float32))
    ).astype(jnp.bfloat16)
    update = lax.psum(jnp.dot(gated_out, out_weight, preferred_element_type=jnp.float32), "mdl")
    stream = residual.astype(jnp.float32) + update
    normed = (
        stream
        * lax.rsqrt(jnp.mean(stream * stream, axis=-1, keepdims=True) + NORM_EPSILON)
        * norm_gain.astype(jnp.float32)
    ).astype(jnp.bfloat16)
    logits = jnp.dot(
        lax.all_gather(normed, "req", axis=0, tiled=True),
        head_weight,
        preferred_element_type=jnp.float32,
    )
    vocab_width = head_weight.shape[1]
    vocab_start = (req_index * lax.axis_size("mdl") + lax.axis_index("mdl")) * vocab_width
    columns = vocab_start + jnp.arange(vocab_width, dtype=jnp.int32)
    chosen = jnp.sum(jnp.where(targets[:, None] == columns[None, :], logits, 0.0), axis=1)
    local_peak = jnp.max(logits, axis=1)
    row_peak = lax.pmax(local_peak, ("req", "mdl"))
    vocab_weights = jnp.exp(logits - row_peak[:, None])
    vocab_total, moment, chosen = lax.psum(
        (jnp.sum(vocab_weights, axis=1), jnp.sum(vocab_weights * logits, axis=1), chosen),
        ("req", "mdl"),
    )
    log_total = row_peak + jnp.log(vocab_total)
    logprob = lax.dynamic_slice_in_dim(chosen - log_total, req_index * fresh_count, fresh_count)
    entropy = lax.dynamic_slice_in_dim(
        log_total - moment / vocab_total, req_index * fresh_count, fresh_count
    )
    return (logprob, entropy)


def solution(mesh):
    placed = (
        P("req", "mdl"),
        P(None, "req", "mdl"),
        P("req", "mdl"),
        P(None, "req", None, "mdl"),
        P(),
        P(),
        P(),
        P("req", None),
        P("req", None),
        P("mdl", None),
        P(),
        P(None, ("req", "mdl")),
        P(),
    )
    return jax.shard_map(
        body, mesh=mesh, in_specs=placed, out_specs=(P("req"), P("req")), check_vma=False
    )
```

profile of v0, /device:TPU:1, one launch (start us, length us, event | category | flops | bytes accessed | tf_op | source)
XLA Modules:
  0.0 604.8 jit_solution(16562163437523480842)
XLA Ops:
  7.2 0.9 select_reduce_fusion.5
  8.1 0.8 fusion.49
  9.2 0.9 select_reduce_fusion.4
  10.2 0.6 gather_fusion
  11.2 6.4 %gather_fusion.1 = bf16[128,2,128,128]{3,2,1,0:T(8,128)(2,1)} fusion(bf16[2,34,128,128]{3,2,1,0:T(8,128)(2,1)S(1)} %copy-done, s32[1024]{0:T(1024)S(1)} %pad_clamp_fusion), kind=kCustom, calls=%fused_computation.1 | custom fusion | bytes 16777728 | tf_op jit(solution)/shard_map/jit(_take)/gather | solution.py:60
  17.6 7.4 %select_bitcast_fusion = bf16[2,128,128,128]{3,2,0,1:T(8,128)(2,1)} fusion(bf16[128,2,128,128]{3,2,1,0:T(8,128)(2,1)} %gather_fusion.1, pred[128]{0:T(512)(128)(4,1)S(1)} %compare_and_fusion), kind=kLoop, calls=%fused_computation.6 | loop fusion | flops 4194304 | bytes 16777344 | tf_op jit(solution)/shard_map/jit(_take)/select_n | solution.py:60
  25.0 15.2 %all-to-all-start = ((bf16[2,128,128,128]{3,2,0,1:T(8,128)(2,1)}), bf16[2,128,128,128]{3,2,0,1:T(8,128)(2,1)}, u32[]{:S(2)}, u32[]{:S(2)}) async-start(bf16[2,128,128,128]{3,2,0,1:T(8,128)(2,1)} %select_bitcast_fusion), calls=%async_computation | async-start | bytes 16777216 | tf_op jit(solution)/shard_map/all_to_all | solution.py:61
  40.2 0.6 dynamic_slice.9
  44.0 0.7 bitcast_select_fusion.1
  45.8 180.1 %all-to-all-done = bf16[2,128,128,128]{3,2,0,1:T(8,128)(2,1)} async-done(((bf16[2,128,128,128]{3,2,0,1:T(8,128)(2,1)}), bf16[2,128,128,128]{3,2,0,1:T(8,128)(2,1)}, u32[]{:S(2)}, u32[]{:S(2)}) %all-to-all-start) | async-done | bytes 8388640 | tf_op jit(solution)/shard_map/all_to_all | solution.py:61
  225.9 4.0 fusion.50
  230.0 2.7 fusion.51
  232.8 0.7 fusion.3
  233.6 1.0 fusion.16
  234.8 0.9 fusion.33
  235.8 69.1 %all-reduce.3.cloned.1.call-done = f32[24,2048]{1,0:T(8,128)} async-done(((f32[24,2048]{1,0:T(8,128)}), f32[24,2048]{1,0:T(8,128)}) %all-reduce.3.cloned.1.call-update) | async-done | bytes 196624 | tf_op jit(solution)/shard_map/psum | solution.py:105
  305.0 1.1 multiply_reduce_fusion.1
  306.1 1.6 multiply_convert_fusion
  307.8 91.5 %all-gather.2.cloned.1.call-done = bf16[1536,2048]{1,0:T(8,128)(2,1)} async-done(((bf16[24,2048]{1,0:T(8,128)(2,1)}), bf16[1536,2048]{1,0:T(8,128)(2,1)}) %all-gather.2.cloned.1.call-update) | async-done | bytes 6291472 | tf_op jit(solution)/shard_map/all_gather | solution.py:113
  399.3 5.8 fusion.53
  405.1 95.8 %pmax.7 = f32[1536]{0:T(1024)S(1)} all-reduce(f32[1536]{0:T(1024)S(1)} %get-tuple-element.42), channel_id=1, replica_groups=mesh['req'=64,'mdl'=8] {'req','mdl'}, use_global_device_ids=true, to_apply=%region_16.17 | all-reduce | flops 1536 | bytes 12288 | tf_op jit(solution)/shard_map/pmax | solution.py:122
  500.9 1.9 multiply_reduce_fusion
  502.8 94.5 %all-reduce = (f32[1536]{0:T(1024)S(1)}, f32[1536]{0:T(1024)S(1)}, f32[1536]{0:T(1024)S(1)}) all-reduce(f32[1536]{0:T(1024)S(1)} %get-tuple-element.26, f32[1536]{0:T(1024)S(1)} %get-tuple-element.25, f32[1536]{0:T(1024)S(1)} %get-tuple-element.24), channel_id=1, replica_groups=mesh['req'=64,'mdl'=8] {'req','mdl'}, use_global_device_ids=true, to_apply=%region_14.15 | all-reduce | flops 4608 | bytes 36864 | tf_op jit(solution)/shard_map/psum | solution.py:124
  597.4 0.6 fusion.47
  (57 shorter events, 3.0 us)
Async XLA Ops:
  7.2 4.1 copy-start
  25.0 17.8 %copy-start.10 = (s32[64]{0:T(128)S(1)}, s32[64]{0:T(128)}, u32[]{:S(2)}) copy-start(s32[64]{0:T(128)} %param.18) | copy-start | bytes 772
  25.0 20.4 %copy-start.8 = (s32[1,24]{1,0:T(1,128)S(1)}, s32[1,24]{1,0:T(1,128)}, u32[]{:S(2)}) copy-start(s32[1,24]{1,0:T(1,128)} %param.20) | copy-start | bytes 292
  25.0 20.5 %copy-start.3 = (bf16[24,256]{1,0:T(8,128)(2,1)S(1)}, bf16[24,256]{1,0:T(8,128)(2,1)}, u32[]{:S(2)}) copy-start(bf16[24,256]{1,0:T(8,128)(2,1)} %param.13) | copy-start | bytes 36868
  25.0 20.5 %copy-start.7 = (bf16[2,24,128]{2,1,0:T(8,128)(2,1)S(1)}, bf16[2,24,128]{2,1,0:T(8,128)(2,1)}, u32[]{:S(2)}) copy-start(bf16[2,24,128]{2,1,0:T(8,128)(2,1)} %param.14) | copy-start | bytes 36868
  25.0 200.9 %all-to-all-start = ((bf16[2,128,128,128]{3,2,0,1:T(8,128)(2,1)}), bf16[2,128,128,128]{3,2,0,1:T(8,128)(2,1)}, u32[]{:S(2)}, u32[]{:S(2)}) async-start(bf16[2,128,128,128]{3,2,0,1:T(8,128)(2,1)} %select_bitcast_fusion), calls=%async_computation | async-start | bytes 16777216 | tf_op jit(solution)/shard_map/all_to_all | solution.py:61
  40.2 264.8 %all-reduce.3.cloned.1.call-start = ((), (), s32[]{:S(2)}) async-start(), calls=%async_computation.1 | async-start | bytes 393216 | tf_op jit(solution)/shard_map/psum | solution.py:105
  233.6 1.2 copy-start.1
  233.6 1.2 copy-start.4
  233.6 2.2 copy-start.6
  233.6 71.4 %copy-start.2 = (bf16[24,2048]{1,0:T(8,128)(2,1)S(1)}, bf16[24,2048]{1,0:T(8,128)(2,1)}, u32[]{:S(2)}) copy-start(bf16[24,2048]{1,0:T(8,128)(2,1)} %param.21) | copy-start | bytes 294916
  233.6 165.7 %copy-start.9 = (bf16[2048,256]{1,0:T(8,128)(2,1)S(1)}, bf16[2048,256]{1,0:T(8,128)(2,1)}, u32[]{:S(2)}) copy-start(bf16[2048,256]{1,0:T(8,128)(2,1)} %param.24) | copy-start | bytes 3145732
  235.8 163.5 %all-gather.2.cloned.1.call-start = ((), (), s32[]{:S(2)}) async-start(), calls=%async_computation.2 | async-start | bytes 6389760 | tf_op jit(solution)/shard_map/all_gather | solution.py:113
  307.7 193.2 %copy-start.5 = (s32[1536]{0:T(1024)S(1)}, s32[1536]{0:T(1024)}, u32[]{:S(2)}) copy-start(s32[1536]{0:T(1024)} %param.25) | copy-start | bytes 18436
Sparse Core Ops, SparseCore 0:
  235.9 69.0 all-reduce.2
  308.3 90.9 all-gather.1
where the time goes:
time: 605 us
  waiting for transfers between devices  341 us (56%)
  blocking collectives  190 us (31%)
  other arithmetic  17.7 us (3%)
  between operations  16.9 us (3%)
  starting transfers between devices  15.2 us (3%)
  local copies, waits for them, and re-layouts  13 us (2%)
  matrix products  10.7 us (2%)
    all_to_all x1, waiting for transfers between devices, body(): lax.all_to_all(outgoing, 'req', split_axis=1, concat_axis=1, tiled=True)  180 us
    pmax x1, blocking collectives, body(): row_peak = lax.pmax(local_peak, ('req', 'mdl'))  95.8 us
    psum x1, blocking collectives, body(): lax.psum((jnp.sum(vocab_weights, axis=1), jnp.sum(vocab_weights * logits,...  94.5 us
    all_gather x1, waiting for transfers between devices, body(): lax.all_gather(normed, 'req', axis=0, tiled=True)  91.5 us
    psum x1, waiting for transfers between devices, body(): lax.psum(jnp.dot(gated_out, out_weight, preferred_element_type=jnp.float3...  69.1 us
    all_to_all x1, starting transfers between devices, body(): lax.all_to_all(outgoing, 'req', split_axis=1, concat_axis=1, tiled=True)  15.2 us
  transfers between devices with their start and end apart: 3, of which 3 were waited for; matrix products, arithmetic and copies ran while one was open for 0% of the time, Pallas kernels for 0%

commit v1 on v0

--- a/solution.py
+++ b/solution.py
@@ -102,7 +102,10 @@
     gated_out = (
         attended.reshape(fresh_count, -1) * jax.nn.sigmoid(gate_logits.astype(jnp.float32))
     ).astype(jnp.bfloat16)
-    update = lax.psum(jnp.dot(gated_out, out_weight, preferred_element_type=jnp.float32), "mdl")
+    update = jnp.sum(
+        lax.all_gather(jnp.dot(gated_out, out_weight, preferred_element_type=jnp.float32), "mdl"),
+        axis=0,
+    )
     stream = residual.astype(jnp.float32) + update
     normed = (
         stream

time: 605 us -> 570 us (0.942)
  waiting for transfers between devices: 341 us -> 305 us
    psum x1 -> x0, waiting for transfers between devices: 69.1 us -> none  [body(): lax.psum(jnp.dot(gated_out, out_weight, preferred_element_type=jnp.float3...]
    all_gather x0 -> x1, waiting for transfers between devices: none -> 34.3 us  [body(): lax.all_gather(jnp.dot(gated_out, out_weight, preferred_element_type=jnp....]
  transfers between devices with their start and end apart: 3 -> 3, of which waited for: 3 -> 3; matrix products, arithmetic and copies ran while one was open for 0% -> 1% of each run, Pallas kernels for 0% -> 0%
where the time goes in v1:
time: 570 us; the launch traced here: 569 us
  waiting for transfers between devices  305 us (54%)
  blocking collectives  190 us (33%)
  other arithmetic  17.4 us (3%)
  between operations  16.9 us (3%)
  starting transfers between devices  15.2 us (3%)
  local copies, waits for them, and re-layouts  13 us (2%)
  matrix products  10.9 us (2%)
    all_to_all x1, waiting for transfers between devices, body(): lax.all_to_all(outgoing, 'req', split_axis=1, concat_axis=1, tiled=True)  180 us
    pmax x1, blocking collectives, body(): row_peak = lax.pmax(local_peak, ('req', 'mdl'))  95.8 us
    psum x1, blocking collectives, body(): lax.psum((jnp.sum(vocab_weights, axis=1), jnp.sum(vocab_weights * logits,...  94.5 us
    all_gather x1, waiting for transfers between devices, body(): lax.all_gather(normed, 'req', axis=0, tiled=True)  91 us
    all_gather x1, waiting for transfers between devices, body(): lax.all_gather(jnp.dot(gated_out, out_weight, preferred_element_type=jnp....  34.3 us
    all_to_all x1, starting transfers between devices, body(): lax.all_to_all(outgoing, 'req', split_axis=1, concat_axis=1, tiled=True)  15.2 us
  transfers between devices with their start and end apart: 3, of which 3 were waited for; matrix products, arithmetic and copies ran while one was open for 1% of the time, Pallas kernels for 0%

profile of v1, /device:TPU:1, one launch (start us, length us, event | category | flops | bytes accessed | tf_op | source)
XLA Modules:
  0.0 569.3 jit_solution(10913712047504713068)
XLA Ops:
  7.2 0.9 select_reduce_fusion.5
  8.1 0.8 fusion.49
  9.2 0.9 select_reduce_fusion.4
  10.2 0.6 gather_fusion
  11.2 6.4 %gather_fusion.1 = bf16[128,2,128,128]{3,2,1,0:T(8,128)(2,1)} fusion(bf16[2,34,128,128]{3,2,1,0:T(8,128)(2,1)S(1)} %copy-done, s32[1024]{0:T(1024)S(1)} %pad_clamp_fusion), kind=kCustom, calls=%fused_computation.1 | custom fusion | bytes 16777728 | tf_op jit(solution)/shard_map/jit(_take)/gather | solution.py:60
  17.6 7.4 %select_bitcast_fusion = bf16[2,128,128,128]{3,2,0,1:T(8,128)(2,1)} fusion(bf16[128,2,128,128]{3,2,1,0:T(8,128)(2,1)} %gather_fusion.1, pred[128]{0:T(512)(128)(4,1)S(1)} %compare_and_fusion), kind=kLoop, calls=%fused_computation.6 | loop fusion | flops 4194304 | bytes 16777344 | tf_op jit(solution)/shard_map/jit(_take)/select_n | solution.py:60
  25.0 15.2 %all-to-all-start = ((bf16[2,128,128,128]{3,2,0,1:T(8,128)(2,1)}), bf16[2,128,128,128]{3,2,0,1:T(8,128)(2,1)}, u32[]{:S(2)}, u32[]{:S(2)}) async-start(bf16[2,128,128,128]{3,2,0,1:T(8,128)(2,1)} %select_bitcast_fusion), calls=%async_computation | async-start | bytes 16777216 | tf_op jit(solution)/shard_map/all_to_all | solution.py:61
  40.2 0.6 dynamic_slice.9
  44.0 0.7 bitcast_select_fusion.1
  45.8 180.1 %all-to-all-done = bf16[2,128,128,128]{3,2,0,1:T(8,128)(2,1)} async-done(((bf16[2,128,128,128]{3,2,0,1:T(8,128)(2,1)}), bf16[2,128,128,128]{3,2,0,1:T(8,128)(2,1)}, u32[]{:S(2)}, u32[]{:S(2)}) %all-to-all-start) | async-done | bytes 8388640 | tf_op jit(solution)/shard_map/all_to_all | solution.py:61
  225.9 4.0 fusion.50
  230.0 2.7 fusion.51
  232.8 0.7 fusion.3
  233.6 1.0 fusion.16
  234.8 0.9 fusion.33
  235.8 34.3 %all-gather.6.cloned.1.call-done = f32[192,2048]{1,0:T(8,128)} async-done(((f32[24,2048]{1,0:T(8,128)}), f32[192,2048]{1,0:T(8,128)}) %all-gather.6.cloned.1.call-update) | async-done | bytes 1572880 | tf_op jit(solution)/shard_map/all_gather | solution.py:106
  270.2 1.5 reduce_sum.118
  271.8 0.7 multiply_convert_fusion
  272.6 91.0 %all-gather.4.cloned.1.call-done = bf16[1536,2048]{1,0:T(8,128)(2,1)} async-done(((bf16[24,2048]{1,0:T(8,128)(2,1)}), bf16[1536,2048]{1,0:T(8,128)(2,1)}) %all-gather.4.cloned.1.call-update) | async-done | bytes 6291472 | tf_op jit(solution)/shard_map/all_gather | solution.py:116
  363.6 6.0 %fusion.53 = (f32[1536]{0:T(1024)S(1)}, f32[1536,256]{0,1:T(8,128)}) fusion(bf16[1536,2048]{1,0:T(8,128)(2,1)} %all-gather.4.cloned.1.call-done, bf16[2048,256]{1,0:T(8,128)(2,1)} %param.24), kind=kOutput, calls=%fused_computation.93 | convolution fusion | flops 1611004416 | bytes 8919040 | tf_op jit(solution)/shard_map/dot_general | solution.py:115
  369.6 95.8 %pmax.7 = f32[1536]{0:T(1024)S(1)} all-reduce(f32[1536]{0:T(1024)S(1)} %get-tuple-element.42), channel_id=1, replica_groups=mesh['req'=64,'mdl'=8] {'req','mdl'}, use_global_device_ids=true, to_apply=%region_16.17 | all-reduce | flops 1536 | bytes 12288 | tf_op jit(solution)/shard_map/pmax | solution.py:125
  465.4 1.9 multiply_reduce_fusion
  467.3 94.5 %all-reduce = (f32[1536]{0:T(1024)S(1)}, f32[1536]{0:T(1024)S(1)}, f32[1536]{0:T(1024)S(1)}) all-reduce(f32[1536]{0:T(1024)S(1)} %get-tuple-element.26, f32[1536]{0:T(1024)S(1)} %get-tuple-element.25, f32[1536]{0:T(1024)S(1)} %get-tuple-element.24), channel_id=1, replica_groups=mesh['req'=64,'mdl'=8] {'req','mdl'}, use_global_device_ids=true, to_apply=%region_14.15 | all-reduce | flops 4608 | bytes 36864 | tf_op jit(solution)/shard_map/psum | solution.py:127
  561.9 0.6 fusion.47
  (56 shorter events, 3.2 us)
Async XLA Ops:
  7.2 4.1 copy-start
  25.0 17.8 %copy-start.9 = (s32[64]{0:T(128)S(1)}, s32[64]{0:T(128)}, u32[]{:S(2)}) copy-start(s32[64]{0:T(128)} %param.18) | copy-start | bytes 772
  25.0 20.4 %copy-start.8 = (s32[1,24]{1,0:T(1,128)S(1)}, s32[1,24]{1,0:T(1,128)}, u32[]{:S(2)}) copy-start(s32[1,24]{1,0:T(1,128)} %param.20) | copy-start | bytes 292
  25.0 20.5 %copy-start.3 = (bf16[24,256]{1,0:T(8,128)(2,1)S(1)}, bf16[24,256]{1,0:T(8,128)(2,1)}, u32[]{:S(2)}) copy-start(bf16[24,256]{1,0:T(8,128)(2,1)} %param.13) | copy-start | bytes 36868
  25.0 20.5 %copy-start.7 = (bf16[2,24,128]{2,1,0:T(8,128)(2,1)S(1)}, bf16[2,24,128]{2,1,0:T(8,128)(2,1)}, u32[]{:S(2)}) copy-start(bf16[2,24,128]{2,1,0:T(8,128)(2,1)} %param.14) | copy-start | bytes 36868
  25.0 200.9 %all-to-all-start = ((bf16[2,128,128,128]{3,2,0,1:T(8,128)(2,1)}), bf16[2,128,128,128]{3,2,0,1:T(8,128)(2,1)}, u32[]{:S(2)}, u32[]{:S(2)}) async-start(bf16[2,128,128,128]{3,2,0,1:T(8,128)(2,1)} %select_bitcast_fusion), calls=%async_computation | async-start | bytes 16777216 | tf_op jit(solution)/shard_map/all_to_all | solution.py:61
  40.2 230.0 %all-gather.6.cloned.1.call-start = ((), (), s32[]{:S(2)}) async-start(), calls=%async_computation.2 | async-start | bytes 1769472 | tf_op jit(solution)/shard_map/all_gather | solution.py:106
  233.6 1.2 copy-start.1
  233.6 1.2 copy-start.4
  233.6 2.2 copy-start.6
  234.6 37.1 %copy-start.2 = (bf16[24,2048]{1,0:T(8,128)(2,1)S(1)}, bf16[24,2048]{1,0:T(8,128)(2,1)}, u32[]{:S(2)}) copy-start(bf16[24,2048]{1,0:T(8,128)(2,1)} %param.21) | copy-start | bytes 294916
  235.8 127.8 %all-gather.4.cloned.1.call-start = ((), (), s32[]{:S(2)}) async-start(), calls=%async_computation.1 | async-start | bytes 6389760 | tf_op jit(solution)/shard_map/all_gather | solution.py:116
  272.6 192.8 %copy-start.5 = (s32[1536]{0:T(1024)S(1)}, s32[1536]{0:T(1024)}, u32[]{:S(2)}) copy-start(s32[1536]{0:T(1024)} %param.25) | copy-start | bytes 18436
Sparse Core Ops, SparseCore 0:
  235.9 34.2 all-gather.5
  273.5 90.0 all-gather.3
